TPU v7x, 256 devices: a whole 4x4x8 slice. The times are simulated.
256 devices in a mesh: pb: 8 (over y, core), kv: 32 (over z, x).
Axes of the slice: x: 4, y: 4, z: 8, core: 2. Of those that a mesh axis runs over, the one named last changes fastest.
Arguments:
- queries: bfloat16 [65536, 4096], P(('pb', 'kv')), may hold values from -6 to 6
- keys: bfloat16 [8192, 4096], P(('pb', 'kv')), may hold values from -6 to 6
- values: bfloat16 [8192, 4096], P(('pb', 'kv')), may hold values from -6 to 6
- key_lists: int32 [512, 8], P('pb'), may hold values from 0 to 63, as said below
- counts: int32 [512], P('pb'), may hold values from 1 to 8, as said below
Outputs:
- attended: bfloat16 [65536, 4096], P(('pb', 'kv'))
Inputs may be any that keep to these rules, and one draw needn't show every extreme that they name: For every query block the first counts entries of its row of key_lists name different key blocks; entries past counts are valid block numbers that do not take part. `counts`: some query block uses all 8 entries of its list.
All inputs are finite; a program needn't handle non-finite values.
Results may differ from a plain program's by a relative error of at most 0.011.
Values may be sent and summed in bfloat16 or wider, within the bound.
No kernel may reach another device: no remote copies, remote signals or barrier semaphores. Data moves between devices by JAX's collectives and lax.ppermute only.
A program may use at most 64 MiB of HBM per device.

v0:
```python
import math
import jax
import jax.numpy as jnp
from jax import lax
from jax.sharding import PartitionSpec as P

HEADS = 32
HD = 128
BLK = 128
MOST = 8


def regroup(split_array, kv_count, pb_count):
    tokens_each = split_array.shape[0] // (kv_count * pb_count)
    shaped = split_array.reshape(kv_count, pb_count, tokens_each, split_array.shape[1])
    return shaped.transpose(1, 0, 2, 3).reshape(-1, split_array.shape[1])


def per_device(queries, keys, values, key_lists, counts):
    kv_count = lax.axis_size("kv")
    pb_count = lax.axis_size("pb")
    head_local = HEADS // kv_count
    scaling = HD ** (-0.5)
    key_whole, value_whole = (
        lax.all_gather(keys, "pb", axis=0, tiled=True),
        lax.all_gather(values, "pb", axis=0, tiled=True),
    )
    key_split, value_split = (
        lax.all_to_all(key_whole, "kv", split_axis=1, concat_axis=0, tiled=True),
        lax.all_to_all(value_whole, "kv", split_axis=1, concat_axis=0, tiled=True),
    )
    key_heads = regroup(key_split, kv_count, pb_count)
    value_heads = regroup(value_split, kv_count, pb_count)
    key_blocks = key_heads.reshape(-1, BLK, head_local, HD)
    value_blocks = value_heads.reshape(-1, BLK, head_local, HD)
    slot_of_key = jnp.arange(MOST * BLK, dtype=jnp.int32) // BLK

    def padded_group(item):
        group_queries, group_lists, group_counts = item
        members = group_queries.shape[0]
        listed_keys = key_blocks[group_lists].reshape(members, MOST * BLK, head_local, HD)
        listed_values = value_blocks[group_lists].reshape(members, MOST * BLK, head_local, HD)
        scores = (
            jnp.einsum(
                "gqhd,gkhd->ghqk", group_queries, listed_keys, preferred_element_type=jnp.float32
            )
            * scaling
        )
        usable = (slot_of_key[None, :] < group_counts[:, None])[:, None, None, :]
        largest = jnp.max(jnp.where(usable, scores, -jnp.inf), axis=-1, keepdims=True)
        raised = jnp.where(usable, jnp.exp(scores - largest), 0.0)
        totals = jnp.sum(raised, axis=-1, keepdims=True)
        weights = (raised / totals).astype(jnp.bfloat16)
        output = jnp.einsum(
            "ghqk,gkhd->gqhd", weights, listed_values, preferred_element_type=jnp.float32
        )
        return output.astype(jnp.bfloat16)

    query_blocks = queries.reshape(-1, BLK, queries.shape[1])
    exchanged = lax.all_to_all(query_blocks, "kv", split_axis=2, concat_axis=0, tiled=True)
    block_total = exchanged.shape[0]
    rows = exchanged.shape[1]
    per_group = math.gcd(block_total, max(1, 512 // rows))
    group_total = block_total // per_group
    grouped = exchanged.reshape(group_total, per_group, rows, head_local, HD)
    lists_grouped = key_lists.reshape(group_total, per_group, key_lists.shape[1])
    counts_grouped = counts.reshape(group_total, per_group)
    produced = lax.map(padded_group, (grouped, lists_grouped, counts_grouped))
    joined = produced.reshape(block_total, rows, head_local * HD)
    result = lax.all_to_all(joined, "kv", split_axis=0, concat_axis=2, tiled=True)
    return result.reshape(queries.shape)


def solution(mesh):
    return jax.shard_map(
        per_device,
        mesh=mesh,
        in_specs=(
            P(("pb", "kv"), None),
            P(("pb", "kv"), None),
            P(("pb", "kv"), None),
            P("pb", None),
            P("pb"),
        ),
        out_specs=P(("pb", "kv"), None),
        check_vma=False,
    )
```

profile of v0, /device:TPU:2, one launch (start us, length us, event | category | flops | bytes accessed | tf_op | source)
XLA Modules:
  0.0 411.0 jit_solution(12888155072686574849)
XLA Ops:
  6.5 6.2 %copy.31 = bf16[2,128,4096]{1,0,2:T(2,128)(2,1)} copy(bf16[2,128,4096]{2,1,0:T(8,128)(2,1)} %bitcast.84) | data formatting | bytes 4194304 | tf_op jit(solution)/shard_map/reshape | solution.py:59
  12.7 11.6 %all-to-all-start.1 = ((bf16[2,128,4096]{1,0,2:T(2,128)(2,1)}), bf16[2,128,4096]{1,0,2:T(2,128)(2,1)S(1)}, u32[]{:S(2)}, u32[]{:S(2)}) async-start(bf16[2,128,4096]{1,0,2:T(2,128)(2,1)} %copy.31), calls=%async_computation.1 | async-start | bytes 4194304 | tf_op jit(solution)/shard_map/all_to_all | solution.py:60
  25.1 30.8 %all-gather.5.cloned.1.call-done = bf16[256,4096]{1,0:T(8,128)(2,1)} async-done(((bf16[32,4096]{1,0:T(8,128)(2,1)}), bf16[256,4096]{1,0:T(8,128)(2,1)}) %all-gather.5.cloned.1.call-update) | async-done | bytes 2097168 | tf_op jit(solution)/shard_map/all_gather | solution.py:25
  55.9 4.1 copy.34
  60.0 13.6 %all-to-all-done.1 = bf16[2,128,4096]{1,0,2:T(2,128)(2,1)S(1)} async-done(((bf16[2,128,4096]{1,0,2:T(2,128)(2,1)}), bf16[2,128,4096]{1,0,2:T(2,128)(2,1)S(1)}, u32[]{:S(2)}, u32[]{:S(2)}) %all-to-all-start.1) | async-done | bytes 2097184 | tf_op jit(solution)/shard_map/all_to_all | solution.py:60
  73.6 6.9 %all-to-all-start.2 = ((bf16[256,32,128]{0,2,1:T(8,128)(2,1)}), bf16[256,32,128]{0,2,1:T(8,128)(2,1)}, u32[]{:S(2)}, u32[]{:S(2)}) async-start(bf16[256,32,128]{0,2,1:T(8,128)(2,1)} %bitcast.76), calls=%async_computation.2 | async-start | bytes 4194304 | tf_op jit(solution)/shard_map/all_to_all | solution.py:29
  81.2 30.8 %all-gather.3.cloned.1.call-done = bf16[256,4096]{1,0:T(8,128)(2,1)} async-done(((bf16[32,4096]{1,0:T(8,128)(2,1)}), bf16[256,4096]{1,0:T(8,128)(2,1)}) %all-gather.3.cloned.1.call-update) | async-done | bytes 2097168 | tf_op jit(solution)/shard_map/all_gather | solution.py:26
  112.1 4.1 copy.28
  116.1 12.9 %all-to-all-done.2 = bf16[256,32,128]{0,2,1:T(8,128)(2,1)} async-done(((bf16[256,32,128]{0,2,1:T(8,128)(2,1)}), bf16[256,32,128]{0,2,1:T(8,128)(2,1)}, u32[]{:S(2)}, u32[]{:S(2)}) %all-to-all-start.2) | async-done | bytes 2097184 | tf_op jit(solution)/shard_map/all_to_all | solution.py:29
  129.1 6.7 %all-to-all-start = ((bf16[256,32,128]{0,2,1:T(8,128)(2,1)}), bf16[256,32,128]{0,2,1:T(8,128)(2,1)}, u32[]{:S(2)}, u32[]{:S(2)}) async-start(bf16[256,32,128]{0,2,1:T(8,128)(2,1)} %bitcast.77), calls=%async_computation | async-start | bytes 4194304 | tf_op jit(solution)/shard_map/all_to_all | solution.py:30
  137.7 4.1 copy.33
  141.7 4.1 copy.35
  147.8 37.0 %all-to-all-done = bf16[256,32,128]{0,2,1:T(8,128)(2,1)} async-done(((bf16[256,32,128]{0,2,1:T(8,128)(2,1)}), bf16[256,32,128]{0,2,1:T(8,128)(2,1)}, u32[]{:S(2)}, u32[]{:S(2)}) %all-to-all-start) | async-done | bytes 2097184 | tf_op jit(solution)/shard_map/all_to_all | solution.py:30
  184.8 4.1 copy.29
  188.9 3.4 copy.30
  192.2 154.8 %while.11 = (s32[]{:T(128)}, bf16[16,4,128,1,128]{4,2,1,0,3:T(8,128)(2,1)}, s32[16,4,8]{2,1,0:T(4,128)S(1)}, bf16[64,128,1,128]{3,1,0,2:T(8,128)(2,1)}, s32[16,4...) while((s32[]{:T(128)}, ...), condition=%wide.region_3.4_spmd.clone, body=%wide.region_0.3_spmd.clone.sunk | while | flops 272709728 | bytes 15493133 | solution.py:68
  196.5 2.3 gather_fusion
  206.2 2.3 gather_fusion
  215.9 2.3 gather_fusion
  225.6 2.3 gather_fusion
  235.2 2.3 gather_fusion
  244.9 2.3 gather_fusion
  254.6 2.3 gather_fusion
  264.3 2.3 gather_fusion
  273.9 2.3 gather_fusion
  283.6 2.3 gather_fusion
  293.3 2.3 gather_fusion
  302.9 2.3 gather_fusion
  312.6 2.3 gather_fusion
  322.3 2.3 gather_fusion
  332.0 2.3 gather_fusion
  347.0 53.5 %all_to_all.62 = bf16[64,128,128]{2,1,0:T(8,128)(2,1)S(1)} all-to-all(bf16[64,128,128]{2,1,0:T(8,128)(2,1)} %bitcast.85), channel_id=1, replica_groups=mesh['pb'=8,'kv'=32] {'kv'}, dimensions={0} | all-to-all | bytes 4194304 | tf_op jit(solution)/shard_map/all_to_all | solution.py:70
  (208 shorter events, 127.9 us)
Async XLA Ops:
  12.7 60.9 %all-to-all-start.1 = ((bf16[2,128,4096]{1,0,2:T(2,128)(2,1)}), bf16[2,128,4096]{1,0,2:T(2,128)(2,1)S(1)}, u32[]{:S(2)}, u32[]{:S(2)}) async-start(bf16[2,128,4096]{1,0,2:T(2,128)(2,1)} %copy.31), calls=%async_computation.1 | async-start | bytes 4194304 | tf_op jit(solution)/shard_map/all_to_all | solution.py:60
  24.3 31.6 %all-gather.5.cloned.1.call-start = ((), (), s32[]{:S(2)}) async-start(), calls=%async_computation.5 | async-start | bytes 2359296 | tf_op jit(solution)/shard_map/all_gather | solution.py:25
  73.6 55.5 %all-to-all-start.2 = ((bf16[256,32,128]{0,2,1:T(8,128)(2,1)}), bf16[256,32,128]{0,2,1:T(8,128)(2,1)}, u32[]{:S(2)}, u32[]{:S(2)}) async-start(bf16[256,32,128]{0,2,1:T(8,128)(2,1)} %bitcast.76), calls=%async_computation.2 | async-start | bytes 4194304 | tf_op jit(solution)/shard_map/all_to_all | solution.py:29
  80.5 31.6 %all-gather.3.cloned.1.call-start = ((), (), s32[]{:S(2)}) async-start(), calls=%async_computation.4 | async-start | bytes 2359296 | tf_op jit(solution)/shard_map/all_gather | solution.py:26
  129.1 6.8 %copy-start = (s32[64,8]{0,1:T(8,128)S(1)}, s32[64,8]{0,1:T(8,128)}, u32[]{:S(2)}) copy-start(s32[64,8]{0,1:T(8,128)} %param.10) | copy-start | bytes 6148
  129.1 6.9 %copy-start.1 = (s32[64]{0:T(128)S(1)}, s32[64]{0:T(128)}, u32[]{:S(2)}) copy-start(s32[64]{0:T(128)} %param.11) | copy-start | bytes 772
  129.1 55.7 %all-to-all-start = ((bf16[256,32,128]{0,2,1:T(8,128)(2,1)}), bf16[256,32,128]{0,2,1:T(8,128)(2,1)}, u32[]{:S(2)}, u32[]{:S(2)}) async-start(bf16[256,32,128]{0,2,1:T(8,128)(2,1)} %bitcast.77), calls=%async_computation | async-start | bytes 4194304 | tf_op jit(solution)/shard_map/all_to_all | solution.py:30
Sparse Core Ops, SparseCore 0:
  27.0 28.8 all-gather.4
  83.2 28.8 all-gather.2
where the time goes:
time: 413 us; the launch traced here: 411 us
  waiting for transfers between devices  127 us (31%)
  local copies, waits for them, and re-layouts  101 us (24%)
  matrix products  56.6 us (14%)
  blocking collectives  53.5 us (13%)
  other arithmetic  33.6 us (8%)
  starting transfers between devices  25.4 us (6%)
  between operations  13.5 us (3%)
    all_to_all x1, blocking collectives, per_device(): lax.all_to_all(joined, 'kv', split_axis=0, concat_axis=2, tiled=True)  53.5 us
    gather x16, local copies, waits for them, and re-layouts, padded_group(): value_blocks[group_lists].reshape(members, MOST * BLK, head_local, HD)  37.4 us
    all_to_all x1, waiting for transfers between devices, per_device(): lax.all_to_all(value_whole, 'kv', split_axis=1, concat_axis=0, tiled=True)  37 us
    dot_general x16, matrix products, padded_group(): jnp.einsum('ghqk,gkhd->gqhd', weights, listed_values, preferred_element_t...  35.1 us
    sub x16, other arithmetic, padded_group(): raised = jnp.where(usable, jnp.exp(scores - largest), 0.0)  32.1 us
    all_gather x1, waiting for transfers between devices, per_device(): lax.all_gather(keys, 'pb', axis=0, tiled=True)  30.8 us
    all_gather x1, waiting for transfers between devices, per_device(): lax.all_gather(values, 'pb', axis=0, tiled=True)  30.8 us
    dot_general x16, matrix products, padded_group(): jnp.einsum('gqhd,gkhd->ghqk', group_queries, listed_keys, preferred_eleme...  21.5 us
  transfers between devices with their start and end apart: 5, of which 5 were waited for; matrix products, arithmetic and copies ran while one was open for 5% of the time, Pallas kernels for 0%

commit v1 on v0

--- a/solution.py
+++ b/solution.py
@@ -23,7 +23,9 @@
     scaling = HD ** (-0.5)
     key_whole, value_whole = (
         lax.all_gather(keys, "pb", axis=0, tiled=True),
-        lax.all_gather(values, "pb", axis=0, tiled=True),
+        jnp.concatenate(
+            lax.all_to_all(jnp.stack([values] * lax.axis_size("pb")), "pb", 0, 0), axis=0
+        ),
     )
     key_split, value_split = (
         lax.all_to_all(key_whole, "kv", split_axis=1, concat_axis=0, tiled=True),

time: 413 us -> 441 us (1.068)
  waiting for transfers between devices: 127 us -> 151 us
    all_to_all x1, waiting for transfers between devices: 13.6 us -> 44.9 us  [per_device(): lax.all_to_all(query_blocks, 'kv', split_axis=2, concat_axis=0, tiled=True)]
    all_gather x1 -> x0, waiting for transfers between devices: 30.8 us -> none  [per_device(): lax.all_gather(values, 'pb', axis=0, tiled=True)]
    all_to_all x1, waiting for transfers between devices: 12.9 us -> 39.6 us  [per_device(): lax.all_to_all(key_whole, 'kv', split_axis=1, concat_axis=0, tiled=True)]
    gather x16, local copies, waits for them, and re-layouts: 12 us -> 37.4 us  [padded_group(): key_blocks[group_lists].reshape(members, MOST * BLK, head_local, HD)]
    gather x16, local copies, waits for them, and re-layouts: 37.4 us -> 11.9 us  [padded_group(): value_blocks[group_lists].reshape(members, MOST * BLK, head_local, HD)]
    all_to_all x1, waiting for transfers between devices: 37 us -> 15.6 us  [per_device(): lax.all_to_all(value_whole, 'kv', split_axis=1, concat_axis=0, tiled=True)]
    all_to_all x0 -> x1, waiting for transfers between devices: none -> 21 us  [per_device(): lax.all_to_all(jnp.stack([values] * lax.axis_size('pb')), 'pb', 0, 0)]
    all_to_all x0 -> x1, starting transfers between devices: none -> 4.47 us  [per_device(): lax.all_to_all(jnp.stack([values] * lax.axis_size('pb')), 'pb', 0, 0)]
where the time goes in v1:
time: 441 us; the launch traced here: 439 us
  waiting for transfers between devices  151 us (34%)
  local copies, waits for them, and re-layouts  101 us (23%)
  matrix products  56.6 us (13%)
  blocking collectives  54 us (12%)
  other arithmetic  33.7 us (8%)
  starting transfers between devices  28.8 us (7%)
  between operations  13.5 us (3%)
    all_to_all x1, blocking collectives, per_device(): lax.all_to_all(joined, 'kv', split_axis=0, concat_axis=2, tiled=True)  54 us
    all_to_all x1, waiting for transfers between devices, per_device(): lax.all_to_all(query_blocks, 'kv', split_axis=2, concat_axis=0, tiled=True)  44.9 us
    all_to_all x1, waiting for transfers between devices, per_device(): lax.all_to_all(key_whole, 'kv', split_axis=1, concat_axis=0, tiled=True)  39.6 us
    gather x16, local copies, waits for them, and re-layouts, padded_group(): key_blocks[group_lists].reshape(members, MOST * BLK, head_local, HD)  37.4 us
    dot_general x16, matrix products, padded_group(): jnp.einsum('ghqk,gkhd->gqhd', weights, listed_values, preferred_element_t...  35.1 us
    sub x16, other arithmetic, padded_group(): raised = jnp.where(usable, jnp.exp(scores - largest), 0.0)  32.2 us
    all_gather x1, waiting for transfers between devices, per_device(): lax.all_gather(keys, 'pb', axis=0, tiled=True)  28.8 us
    dot_general x16, matrix products, padded_group(): jnp.einsum('gqhd,gkhd->ghqk', group_queries, listed_keys, preferred_eleme...  21.4 us
  transfers between devices with their start and end apart: 5, of which 5 were waited for; matrix products, arithmetic and copies ran while one was open for 5% of the time, Pallas kernels for 0%

profile of v1, /device:TPU:2, one launch (start us, length us, event | category | flops | bytes accessed | tf_op | source)
XLA Modules:
  0.0 439.1 jit_solution(14084261264104227928)
XLA Ops:
  6.5 2.5 stack.2
  9.0 4.5 %all-to-all-start = ((bf16[8,32,4096]{2,1,0:T(8,128)(2,1)}), bf16[8,32,4096]{2,1,0:T(8,128)(2,1)S(1)}, u32[]{:S(2)}, u32[]{:S(2)}) async-start(bf16[8,32,4096]{2,1,0:T(8,128)(2,1)} %stack.2), calls=%async_computation | async-start | bytes 4194304 | tf_op jit(solution)/shard_map/all_to_all | solution.py:27
  13.5 6.2 %copy.29 = bf16[2,128,4096]{1,0,2:T(2,128)(2,1)} copy(bf16[2,128,4096]{2,1,0:T(8,128)(2,1)} %bitcast.87) | data formatting | bytes 4194304 | tf_op jit(solution)/shard_map/reshape | solution.py:61
  19.7 21.0 %all-to-all-done = bf16[8,32,4096]{2,1,0:T(8,128)(2,1)S(1)} async-done(((bf16[8,32,4096]{2,1,0:T(8,128)(2,1)}), bf16[8,32,4096]{2,1,0:T(8,128)(2,1)S(1)}, u32[]{:S(2)}, u32[]{:S(2)}) %all-to-all-start) | async-done | bytes 2097184 | tf_op jit(solution)/shard_map/all_to_all | solution.py:27
  42.0 11.6 %all-to-all-start.2 = ((bf16[2,128,4096]{1,0,2:T(2,128)(2,1)}), bf16[2,128,4096]{1,0,2:T(2,128)(2,1)S(1)}, u32[]{:S(2)}, u32[]{:S(2)}) async-start(bf16[2,128,4096]{1,0,2:T(2,128)(2,1)} %copy.29), calls=%async_computation.2 | async-start | bytes 4194304 | tf_op jit(solution)/shard_map/all_to_all | solution.py:62
  57.9 44.9 %all-to-all-done.2 = bf16[2,128,4096]{1,0,2:T(2,128)(2,1)S(1)} async-done(((bf16[2,128,4096]{1,0,2:T(2,128)(2,1)}), bf16[2,128,4096]{1,0,2:T(2,128)(2,1)S(1)}, u32[]{:S(2)}, u32[]{:S(2)}) %all-to-all-start.2) | async-done | bytes 2097184 | tf_op jit(solution)/shard_map/all_to_all | solution.py:62
  102.7 6.9 %all-to-all-start.1 = ((bf16[256,32,128]{2,0,1:T(8,128)(2,1)}), bf16[256,32,128]{2,0,1:T(8,128)(2,1)}, u32[]{:S(2)}, u32[]{:S(2)}) async-start(bf16[256,32,128]{2,0,1:T(8,128)(2,1)} %copy.27), calls=%async_computation.1 | async-start | bytes 4194304 | tf_op jit(solution)/shard_map/all_to_all | solution.py:32
  110.4 28.8 %all-gather.2.cloned.1.call-done = bf16[256,4096]{1,0:T(8,128)(2,1)} async-done(((bf16[32,4096]{1,0:T(8,128)(2,1)}), bf16[256,4096]{1,0:T(8,128)(2,1)}) %all-gather.2.cloned.1.call-update) | async-done | bytes 2097168 | tf_op jit(solution)/shard_map/all_gather | solution.py:25
  139.2 4.1 copy.32
  143.3 15.6 %all-to-all-done.1 = bf16[256,32,128]{2,0,1:T(8,128)(2,1)} async-done(((bf16[256,32,128]{2,0,1:T(8,128)(2,1)}), bf16[256,32,128]{2,0,1:T(8,128)(2,1)}, u32[]{:S(2)}, u32[]{:S(2)}) %all-to-all-start.1) | async-done | bytes 2097184 | tf_op jit(solution)/shard_map/all_to_all | solution.py:32
  158.9 5.8 %all-to-all-start.3 = ((bf16[256,32,128]{0,2,1:T(8,128)(2,1)}), bf16[256,32,128]{0,2,1:T(8,128)(2,1)}, u32[]{:S(2)}, u32[]{:S(2)}) async-start(bf16[256,32,128]{0,2,1:T(8,128)(2,1)} %bitcast.79), calls=%async_computation.3 | async-start | bytes 4194304 | tf_op jit(solution)/shard_map/all_to_all | solution.py:31
  166.5 4.1 copy.31
  172.6 39.6 %all-to-all-done.3 = bf16[256,32,128]{0,2,1:T(8,128)(2,1)} async-done(((bf16[256,32,128]{0,2,1:T(8,128)(2,1)}), bf16[256,32,128]{0,2,1:T(8,128)(2,1)}, u32[]{:S(2)}, u32[]{:S(2)}) %all-to-all-start.3) | async-done | bytes 2097184 | tf_op jit(solution)/shard_map/all_to_all | solution.py:31
  212.2 4.1 copy.33
  216.4 3.4 copy.34
  219.7 154.8 %while.11 = (s32[]{:T(128)}, bf16[16,4,128,1,128]{4,2,1,0,3:T(8,128)(2,1)}, s32[16,4,8]{2,1,0:T(4,128)S(1)}, bf16[64,128,1,128]{3,1,0,2:T(8,128)(2,1)S(1)}, s32[...) while((s32[]{:T(128)}, ...), condition=%wide.region_3.4_spmd.clone, body=%wide.region_0.3_spmd.clone.sunk | while | flops 272709728 | bytes 15493133 | solution.py:70
  219.8 2.3 gather_fusion.1
  229.5 2.3 gather_fusion.1
  239.2 2.3 gather_fusion.1
  248.9 2.3 gather_fusion.1
  258.5 2.3 gather_fusion.1
  268.2 2.3 gather_fusion.1
  277.9 2.3 gather_fusion.1
  287.6 2.3 gather_fusion.1
  297.2 2.3 gather_fusion.1
  306.9 2.3 gather_fusion.1
  316.6 2.3 gather_fusion.1
  326.3 2.3 gather_fusion.1
  336.0 2.3 gather_fusion.1
  345.6 2.3 gather_fusion.1
  355.3 2.3 gather_fusion.1
  374.6 54.0 %all_to_all.67 = bf16[64,128,128]{2,1,0:T(8,128)(2,1)S(1)} all-to-all(bf16[64,128,128]{2,1,0:T(8,128)(2,1)} %bitcast.88), channel_id=1, replica_groups=mesh['pb'=8,'kv'=32] {'kv'}, dimensions={0} | all-to-all | bytes 4194304 | tf_op jit(solution)/shard_map/all_to_all | solution.py:72
  (210 shorter events, 132.7 us)
Async XLA Ops:
  9.0 31.7 %all-to-all-start = ((bf16[8,32,4096]{2,1,0:T(8,128)(2,1)}), bf16[8,32,4096]{2,1,0:T(8,128)(2,1)S(1)}, u32[]{:S(2)}, u32[]{:S(2)}) async-start(bf16[8,32,4096]{2,1,0:T(8,128)(2,1)} %stack.2), calls=%async_computation | async-start | bytes 4194304 | tf_op jit(solution)/shard_map/all_to_all | solution.py:27
  40.7 1.3 copy-start
  42.0 60.7 %all-to-all-start.2 = ((bf16[2,128,4096]{1,0,2:T(2,128)(2,1)}), bf16[2,128,4096]{1,0,2:T(2,128)(2,1)S(1)}, u32[]{:S(2)}, u32[]{:S(2)}) async-start(bf16[2,128,4096]{1,0,2:T(2,128)(2,1)} %copy.29), calls=%async_computation.2 | async-start | bytes 4194304 | tf_op jit(solution)/shard_map/all_to_all | solution.py:62
  102.7 56.2 %all-to-all-start.1 = ((bf16[256,32,128]{2,0,1:T(8,128)(2,1)}), bf16[256,32,128]{2,0,1:T(8,128)(2,1)}, u32[]{:S(2)}, u32[]{:S(2)}) async-start(bf16[256,32,128]{2,0,1:T(8,128)(2,1)} %copy.27), calls=%async_computation.1 | async-start | bytes 4194304 | tf_op jit(solution)/shard_map/all_to_all | solution.py:32
  109.6 29.6 %all-gather.2.cloned.1.call-start = ((), (), s32[]{:S(2)}) async-start(), calls=%async_computation.5 | async-start | bytes 2359296 | tf_op jit(solution)/shard_map/all_gather | solution.py:25
  158.9 5.8 %copy-start.1 = (s32[64,8]{0,1:T(8,128)S(1)}, s32[64,8]{0,1:T(8,128)}, u32[]{:S(2)}) copy-start(s32[64,8]{0,1:T(8,128)} %param.10) | copy-start | bytes 6148
  158.9 5.9 %copy-start.2 = (s32[64]{0:T(128)S(1)}, s32[64]{0:T(128)}, u32[]{:S(2)}) copy-start(s32[64]{0:T(128)} %param.11) | copy-start | bytes 772
  158.9 53.3 %all-to-all-start.3 = ((bf16[256,32,128]{0,2,1:T(8,128)(2,1)}), bf16[256,32,128]{0,2,1:T(8,128)(2,1)}, u32[]{:S(2)}, u32[]{:S(2)}) async-start(bf16[256,32,128]{0,2,1:T(8,128)(2,1)} %bitcast.79), calls=%async_computation.3 | async-start | bytes 4194304 | tf_op jit(solution)/shard_map/all_to_all | solution.py:31
Sparse Core Ops, SparseCore 0:
  112.3 26.8 all-gather.1
